TPU v7x, 32 devices: a whole 2x2x4 slice. The times are simulated.
32 devices in a mesh: row: 4 (over z), col: 8 (over y, x, core).
Axes of the slice: x: 2, y: 2, z: 4, core: 2. Of those that a mesh axis runs over, the one named last changes fastest.
Arguments:
- positions: float32 [3, 4, 8, 64], P(None, 'row', 'col'), may hold values from 0 to 32, as said below
- species: int32 [4, 8, 64], P('row', 'col'), may hold values from 0 to 3
- descriptors: float32 [128, 4, 8, 64], P(None, 'row', 'col'), may hold values from -6 to 6
- readout: float32 [4, 128], replicated, may hold values from -0.5 to 0.5
- hardness: float32 [4], replicated, may hold values from 1 to 4
- widths: float32 [4], replicated, may hold values from 0.5 to 1.5
Outputs:
- charges: float32 [4, 8, 64], P('row', 'col')
- forces: float32 [3, 4, 8, 64], P(None, 'row', 'col')
Inputs may be any that keep to these rules, and one draw needn't show every extreme that they name: `positions`: the atoms of brick (b, c) lie in [4 b, 4 b + 4) x [4 c, 4 c + 4) x [0, 4); no two atoms are closer than 0.4.
All inputs are finite; a program needn't handle non-finite values.
Results may differ from a plain program's by a relative error of at most 0.0003.
Values sent between devices are 32-bit elements; how exact they have to be, the bound alone decides.
No kernel may reach another device: no remote copies, remote signals or barrier semaphores. Data moves between devices by JAX's collectives and lax.ppermute only.
A program may use at most 64 MiB of HBM per device.

v0:
```python
import jax
import jax.numpy as jnp
from jax import lax
from jax.sharding import PartitionSpec as P

ITERS = 3
ROOT_PI = 1.7724538509055159
TWO_ROOT = 1.1283791670955126


def screened(row_geometry, col_geometry, self_pair):
    squared = jnp.zeros(self_pair.shape, row_geometry.dtype)
    for axis_id in range(3):
        separation = row_geometry[axis_id][:, None] - col_geometry[axis_id][None, :]
        squared = squared + separation * separation
    squared = jnp.where(self_pair, 1.0, squared)
    inverse = lax.rsqrt(squared)
    screening = lax.rsqrt(2.0 * (row_geometry[3][:, None] + col_geometry[3][None, :]))
    return jnp.where(self_pair, 0.0, lax.erf(screening * squared * inverse) * inverse)


def pulling(row_geometry, col_geometry, self_pair, col_charges):
    separations = []
    squared = jnp.zeros(self_pair.shape, row_geometry.dtype)
    for axis_id in range(3):
        separation = row_geometry[axis_id][:, None] - col_geometry[axis_id][None, :]
        separations.append(separation)
        squared = squared + separation * separation
    squared = jnp.where(self_pair, 1.0, squared)
    inverse = lax.rsqrt(squared)
    screening = lax.rsqrt(2.0 * (row_geometry[3][:, None] + col_geometry[3][None, :]))
    slope = (
        (
            lax.erf(screening * squared * inverse) * inverse
            - TWO_ROOT * screening * jnp.exp(-screening * screening * squared)
        )
        * inverse
        * inverse
    )
    slope = jnp.where(self_pair, 0.0, slope) * col_charges[None, :]
    return jnp.stack(
        [
            jnp.sum(slope * separations[0], 1),
            jnp.sum(slope * separations[1], 1),
            jnp.sum(slope * separations[2], 1),
        ]
    )


def apply_kernel(row_geometry, col_geometry, self_pair, vectors):
    kernel = screened(row_geometry, col_geometry, self_pair)
    return jnp.sum(kernel[None, :, :] * vectors[:, None, :], 2)


def shards(positions, species, descriptors, readout, hardness, widths):
    per_brick = species.shape[-1]
    row_at = lax.axis_index("row")
    col_at = lax.axis_index("col")
    kind_range = jnp.arange(hardness.shape[0], dtype=jnp.int32)
    onehot = (kind_range[:, None] == species.reshape(1, per_brick)).astype(jnp.float32)
    hard_atom = jnp.sum(onehot * hardness[:, None], 0)
    width_atom = jnp.sum(onehot * widths[:, None], 0)
    features = descriptors.reshape(descriptors.shape[0], per_brick)
    atom_weights = jnp.zeros(features.shape, jnp.float32)
    for kind in range(hardness.shape[0]):
        atom_weights = atom_weights + onehot[kind][None, :] * readout[kind][:, None]
    negativity = jnp.sum(features * atom_weights, 0)
    self_term = hard_atom + 1.0 / (width_atom * ROOT_PI)
    own_geometry = jnp.concatenate(
        [positions, (width_atom * width_atom).reshape(1, 1, 1, per_brick)], 0
    )
    row_geometry = lax.all_gather(own_geometry, "col", axis=2, tiled=True).reshape(4, -1)
    col_geometry = lax.all_gather(own_geometry, "row", axis=1, tiled=True).reshape(4, -1)
    row_total = row_geometry.shape[1]
    block_rows = 512
    block_count = row_total // block_rows

    def pair_mask(row_index, col_index):
        same_slot = (
            row_index[:, None] - col_at * per_brick == col_index[None, :] - row_at * per_brick
        )
        return same_slot & (row_index[:, None] // per_brick == col_at)

    def sweep(segment, block_fn, rows_out):
        columns = segment.shape[-1]
        col_index = jnp.arange(columns, dtype=jnp.int32)

        def one_block(block):
            first_row = block * block_rows
            row_part = lax.dynamic_slice_in_dim(row_geometry, first_row, block_rows, 1)
            row_index = first_row + jnp.arange(block_rows, dtype=jnp.int32)
            return block_fn(row_part, col_geometry, pair_mask(row_index, col_index), segment)

        blocks = lax.map(one_block, jnp.arange(block_count, dtype=jnp.int32))
        return jnp.moveaxis(blocks, 0, 1).reshape(rows_out, row_total)

    def squares(resid):
        return lax.psum(jnp.sum(resid * resid, 1), ("row", "col"))

    rhs = jnp.stack([-negativity, jnp.ones((per_brick,), jnp.float32)])
    solution = jnp.zeros_like(rhs)
    resid = rhs
    direction = rhs
    norm_now = squares(resid)
    for iteration in range(ITERS):
        partial_value = sweep(lax.all_gather(direction, "row", axis=1, tiled=True), apply_kernel, 2)
        whole = lax.psum(partial_value, "col")
        mine = lax.dynamic_slice_in_dim(whole, col_at * per_brick, per_brick, 1)
        image = mine + self_term[None, :] * direction
        curvature = lax.psum(jnp.sum(direction * image, 1), ("row", "col"))
        step_size = norm_now / curvature
        solution = solution + step_size[:, None] * direction
        if iteration + 1 < ITERS:
            resid = resid - step_size[:, None] * image
            norm_next = squares(resid)
            direction = resid + (norm_next / norm_now)[:, None] * direction
            norm_now = norm_next
    totals = lax.psum(jnp.sum(solution, 1), ("row", "col"))
    lagrange = totals[0] / totals[1]
    charges = solution[0] - lagrange * solution[1]
    field_sums = jnp.zeros((3, row_total), jnp.float32) + sweep(
        lax.all_gather(charges, "row", axis=0, tiled=True), pulling, 3
    )
    whole_pull = lax.psum(field_sums, "col")
    mine_pull = lax.dynamic_slice_in_dim(whole_pull, col_at * per_brick, per_brick, 1)
    forces = (charges[None, :] * mine_pull).reshape(3, 1, 1, per_brick)
    return (charges.reshape(1, 1, per_brick), forces)


def solution(mesh):
    in_specs = (
        P(None, "row", "col", None),
        P("row", "col", None),
        P(None, "row", "col", None),
        P(),
        P(),
        P(),
    )
    out_specs = (P("row", "col", None), P(None, "row", "col", None))
    return jax.shard_map(shards, mesh=mesh, in_specs=in_specs, out_specs=out_specs, check_vma=False)
```

profile of v0, /device:TPU:0, one launch (start us, length us, event | category | flops | bytes accessed | tf_op | source)
XLA Modules:
  0.0 359.4 jit_solution(654294700805835680)
XLA Ops:
  0.7 0.6 copy-done.1
  1.4 0.7 copy-done.4
  2.1 10.4 %all_gather.18 = f32[4,1,8,64]{3,0,1,2:T(4,128)S(1)} all-gather(f32[4,1,1,64]{3,0,1,2:T(4,128)S(1)} %pad_maximum_fusion.1), channel_id=1, replica_groups=mesh['row'=4,'col'=8] {'col'}, dimensions={2}, use_global_device_ids=true | all-gather | bytes 9216 | tf_op jit(solution)/shard_map/all_gather | solution.py:72
  12.8 12.1 %all_gather.19 = f32[4,4,1,64]{3,0,2,1:T(4,128)S(1)} all-gather(f32[4,1,1,64]{3,0,2,1:T(4,128)S(1)} %fusion.29), channel_id=1, replica_groups=mesh['row'=4,'col'=8] {'row'}, dimensions={1}, use_global_device_ids=true | all-gather | bytes 5120 | tf_op jit(solution)/shard_map/all_gather | solution.py:73
  25.3 0.5 fusion.12
  25.9 0.7 copy-done.2
  26.5 0.2 fusion.13
  26.7 9.7 %all-gather.1 = f32[4,64,2]{1,2,0:T(2,128)S(1)} all-gather(f32[1,64,2]{1,2,0:T(2,128)S(1)} %pad_bitcast_fusion), channel_id=1, replica_groups=mesh['row'=4,'col'=8] {'row'}, dimensions={0}, use_global_device_ids=true | all-gather | bytes 2560 | tf_op jit(solution)/shard_map/all_gather | solution.py:106
  36.5 0.2 multiply_reduce_fusion.2
  36.7 11.8 %psum.78 = f32[2,512]{1,0:T(2,128)S(1)} all-reduce(f32[2,512]{1,0:T(2,128)S(1)} %multiply_reduce_fusion.2), channel_id=1, replica_groups=mesh['row'=4,'col'=8] {'col'}, use_global_device_ids=true, to_apply=%region_5.6 | all-reduce | flops 1024 | bytes 8192 | tf_op jit(solution)/shard_map/psum | solution.py:107
  48.8 37.6 %all-reduce.2 = (f32[2]{0:T(128)S(1)}, f32[2]{0:T(128)S(1)}) all-reduce(f32[2]{0:T(128)S(1)} %get-tuple-element.86, f32[2]{0:T(128)S(1)} %get-tuple-element.85), channel_id=1, replica_groups=mesh['row'=4,'col'=8] {'row','col'}, use_global_device_ids=true, to_apply=%region_2.0 | all-reduce | flops 4 | bytes 32 | tf_op jit(solution)/shard_map/psum | solution.py:98
  86.4 0.2 multiply_reduce_fusion.6
  86.6 41.6 %psum.80 = f32[2]{0:T(128)S(1)} all-reduce(f32[2]{0:T(128)S(1)} %get-tuple-element.113), channel_id=1, replica_groups=mesh['row'=4,'col'=8] {'row','col'}, use_global_device_ids=true, to_apply=%region_10.11 | all-reduce | flops 2 | bytes 16 | tf_op jit(solution)/shard_map/psum | solution.py:98
  128.3 9.1 %all-gather.2 = f32[4,64,2]{1,2,0:T(2,128)S(1)} all-gather(f32[1,64,2]{1,2,0:T(2,128)S(1)} %fusion.28), channel_id=1, replica_groups=mesh['row'=4,'col'=8] {'row'}, dimensions={0}, use_global_device_ids=true | all-gather | bytes 2560 | tf_op jit(solution)/shard_map/all_gather | solution.py:106
  137.4 0.2 multiply_reduce_fusion.1
  137.7 11.8 %psum.81 = f32[2,512]{1,0:T(2,128)S(1)} all-reduce(f32[2,512]{1,0:T(2,128)S(1)} %multiply_reduce_fusion.1), channel_id=1, replica_groups=mesh['row'=4,'col'=8] {'col'}, use_global_device_ids=true, to_apply=%region_12.13 | all-reduce | flops 1024 | bytes 8192 | tf_op jit(solution)/shard_map/psum | solution.py:107
  149.7 38.5 %psum.82 = f32[2]{0:T(128)S(1)} all-reduce(f32[2]{0:T(128)S(1)} %multiply_reduce_fusion.5), channel_id=1, replica_groups=mesh['row'=4,'col'=8] {'row','col'}, use_global_device_ids=true, to_apply=%region_14.15 | all-reduce | flops 2 | bytes 16 | tf_op jit(solution)/shard_map/psum | solution.py:110
  188.2 0.2 multiply_reduce_fusion.4
  188.4 41.5 %psum.83 = f32[2]{0:T(128)S(1)} all-reduce(f32[2]{0:T(128)S(1)} %get-tuple-element.103), channel_id=1, replica_groups=mesh['row'=4,'col'=8] {'row','col'}, use_global_device_ids=true, to_apply=%region_16.17 | all-reduce | flops 2 | bytes 16 | tf_op jit(solution)/shard_map/psum | solution.py:98
  230.0 9.1 %all-gather.3 = f32[4,64,2]{1,2,0:T(2,128)S(1)} all-gather(f32[1,64,2]{1,2,0:T(2,128)S(1)} %bitcast.57), channel_id=1, replica_groups=mesh['row'=4,'col'=8] {'row'}, dimensions={0}, use_global_device_ids=true | all-gather | bytes 2560 | tf_op jit(solution)/shard_map/all_gather | solution.py:106
  239.2 0.2 multiply_reduce_fusion
  239.4 11.8 %psum.84 = f32[2,512]{1,0:T(2,128)S(1)} all-reduce(f32[2,512]{1,0:T(2,128)S(1)} %multiply_reduce_fusion), channel_id=1, replica_groups=mesh['row'=4,'col'=8] {'col'}, use_global_device_ids=true, to_apply=%region_18.19 | all-reduce | flops 1024 | bytes 8192 | tf_op jit(solution)/shard_map/psum | solution.py:107
  251.4 38.5 %psum.85 = f32[2]{0:T(128)S(1)} all-reduce(f32[2]{0:T(128)S(1)} %multiply_reduce_fusion.3), channel_id=1, replica_groups=mesh['row'=4,'col'=8] {'row','col'}, use_global_device_ids=true, to_apply=%region_20.21 | all-reduce | flops 2 | bytes 16 | tf_op jit(solution)/shard_map/psum | solution.py:110
  289.9 0.2 fusion.25
  290.1 41.5 %psum.86 = f32[2]{0:T(128)S(1)} all-reduce(f32[2]{0:T(128)S(1)} %get-tuple-element.101), channel_id=1, replica_groups=mesh['row'=4,'col'=8] {'row','col'}, use_global_device_ids=true, to_apply=%region_22.23 | all-reduce | flops 2 | bytes 16 | tf_op jit(solution)/shard_map/psum | solution.py:118
  331.7 0.6 fusion.27
  333.6 0.6 copy-done.7
  334.2 0.6 dynamic-slice
  335.6 9.9 %all-reduce.1 = f32[256]{0:T(256)S(1)} all-reduce(f32[256]{0:T(256)S(1)} %get-tuple-element.99), channel_id=2, replica_groups=mesh['row'=4,'col'=8] {'row'}, use_global_device_ids=true, to_apply=%add.1 | all-reduce | flops 256 | bytes 2048
  345.5 1.2 fusion.3
  346.7 12.0 %psum.87 = f32[3,512]{1,0:T(4,128)S(1)} all-reduce(f32[3,512]{1,0:T(4,128)S(1)} %pad_maximum_fusion), channel_id=1, replica_groups=mesh['row'=4,'col'=8] {'col'}, use_global_device_ids=true, to_apply=%region_26.27 | all-reduce | flops 1536 | bytes 12288 | tf_op jit(solution)/shard_map/psum | solution.py:124
  358.8 0.6 reshape.327
  (55 shorter events, 2.1 us)
Async XLA Ops:
  0.6 0.7 copy-start.1
  0.6 0.7 copy-start.6
  0.7 0.7 copy-start.5
  1.4 0.7 copy-start.4
  25.3 1.2 copy-start
  25.8 0.7 copy-start.2
  333.6 0.7 copy-start.7
  335.6 23.2 %copy-start.3 = (f32[1,64]{1,0:T(1,128)}, f32[1,64]{1,0:T(1,128)S(1)}, u32[]{:S(2)}) copy-start(f32[1,64]{1,0:T(1,128)S(1)} %get-tuple-element.100) | copy-start | bytes 772
where the time goes:
time: 361 us; the launch traced here: 359 us
  blocking collectives  347 us (96%)
  local copies, waits for them, and re-layouts  5.38 us (1%)
  other arithmetic  4.18 us (1%)
    psum x3, blocking collectives, squares(): return lax.psum(jnp.sum(resid * resid, 1), ('row', 'col'))  121 us
    psum x2, blocking collectives, shards(): curvature = lax.psum(jnp.sum(direction * image, 1), ('row', 'col'))  77.1 us
    psum x1, blocking collectives, shards(): totals = lax.psum(jnp.sum(solution, 1), ('row', 'col'))  41.5 us
    psum x3, blocking collectives, shards(): whole = lax.psum(partial_value, 'col')  35.4 us
    all_gather x3, blocking collectives, shards(): lax.all_gather(direction, 'row', axis=1, tiled=True)  27.9 us
    all_gather x1, blocking collectives, shards(): lax.all_gather(own_geometry, 'row', axis=1, tiled=True).reshape(4, -1)  12.1 us
    psum x1, blocking collectives, shards(): whole_pull = lax.psum(field_sums, 'col')  12 us
    all_gather x1, blocking collectives, shards(): lax.all_gather(own_geometry, 'col', axis=2, tiled=True).reshape(4, -1)  10.4 us

commit v1 on v0

--- a/solution.py
+++ b/solution.py
@@ -2,6 +2,7 @@
 import jax.numpy as jnp
 from jax import lax
 from jax.sharding import PartitionSpec as P
+from jax.lax import psum
 
 ITERS = 3
 ROOT_PI = 1.7724538509055159
@@ -115,7 +116,9 @@
             norm_next = squares(resid)
             direction = resid + (norm_next / norm_now)[:, None] * direction
             norm_now = norm_next
-    totals = lax.psum(jnp.sum(solution, 1), ("row", "col"))
+    totals = jnp.sum(solution, 1)
+    for to_i in ("col", "row"):
+        totals = psum(totals, to_i)
     lagrange = totals[0] / totals[1]
     charges = solution[0] - lagrange * solution[1]
     field_sums = jnp.zeros((3, row_total), jnp.float32) + sweep(

time: 361 us -> 341 us (0.945)
  blocking collectives: 347 us -> 327 us
    psum x1 -> x2, blocking collectives: 41.5 us -> 22.6 us  [shards(): totals = psum(totals, to_i)]
where the time goes in v1:
time: 341 us; the launch traced here: 339 us
  blocking collectives  327 us (96%)
  local copies, waits for them, and re-layouts  5.38 us (2%)
  other arithmetic  4.18 us (1%)
    psum x3, blocking collectives, squares(): return lax.psum(jnp.sum(resid * resid, 1), ('row', 'col'))  121 us
    psum x2, blocking collectives, shards(): curvature = lax.psum(jnp.sum(direction * image, 1), ('row', 'col'))  77.1 us
    psum x3, blocking collectives, shards(): whole = lax.psum(partial_value, 'col')  35.4 us
    all_gather x3, blocking collectives, shards(): lax.all_gather(direction, 'row', axis=1, tiled=True)  27.9 us
    psum x2, blocking collectives, shards(): totals = psum(totals, to_i)  22.6 us
    all_gather x1, blocking collectives, shards(): lax.all_gather(own_geometry, 'row', axis=1, tiled=True).reshape(4, -1)  12.1 us
    psum x1, blocking collectives, shards(): whole_pull = lax.psum(field_sums, 'col')  12 us
    all_gather x1, blocking collectives, shards(): lax.all_gather(own_geometry, 'col', axis=2, tiled=True).reshape(4, -1)  10.4 us

profile of v1, /device:TPU:0, one launch (start us, length us, event | category | flops | bytes accessed | tf_op | source)
XLA Modules:
  0.0 339.4 jit_solution(16048692008540789038)
XLA Ops:
  0.7 0.6 copy-done.1
  1.4 0.7 copy-done.4
  2.1 10.4 %all_gather.18 = f32[4,1,8,64]{3,0,1,2:T(4,128)S(1)} all-gather(f32[4,1,1,64]{3,0,1,2:T(4,128)S(1)} %pad_maximum_fusion.1), channel_id=1, replica_groups=mesh['row'=4,'col'=8] {'col'}, dimensions={2}, use_global_device_ids=true | all-gather | bytes 9216 | tf_op jit(solution)/shard_map/all_gather | solution.py:73
  12.8 12.1 %all_gather.19 = f32[4,4,1,64]{3,0,2,1:T(4,128)S(1)} all-gather(f32[4,1,1,64]{3,0,2,1:T(4,128)S(1)} %fusion.29), channel_id=1, replica_groups=mesh['row'=4,'col'=8] {'row'}, dimensions={1}, use_global_device_ids=true | all-gather | bytes 5120 | tf_op jit(solution)/shard_map/all_gather | solution.py:74
  25.3 0.5 fusion.12
  25.9 0.7 copy-done.2
  26.5 0.2 fusion.13
  26.7 9.7 %all-gather.1 = f32[4,64,2]{1,2,0:T(2,128)S(1)} all-gather(f32[1,64,2]{1,2,0:T(2,128)S(1)} %pad_bitcast_fusion), channel_id=1, replica_groups=mesh['row'=4,'col'=8] {'row'}, dimensions={0}, use_global_device_ids=true | all-gather | bytes 2560 | tf_op jit(solution)/shard_map/all_gather | solution.py:107
  36.5 0.2 multiply_reduce_fusion.2
  36.7 11.8 %psum.85 = f32[2,512]{1,0:T(2,128)S(1)} all-reduce(f32[2,512]{1,0:T(2,128)S(1)} %multiply_reduce_fusion.2), channel_id=1, replica_groups=mesh['row'=4,'col'=8] {'col'}, use_global_device_ids=true, to_apply=%region_5.6 | all-reduce | flops 1024 | bytes 8192 | tf_op jit(solution)/shard_map/psum | solution.py:108
  48.8 37.6 %all-reduce.2 = (f32[2]{0:T(128)S(1)}, f32[2]{0:T(128)S(1)}) all-reduce(f32[2]{0:T(128)S(1)} %get-tuple-element.86, f32[2]{0:T(128)S(1)} %get-tuple-element.85), channel_id=1, replica_groups=mesh['row'=4,'col'=8] {'row','col'}, use_global_device_ids=true, to_apply=%region_2.0 | all-reduce | flops 4 | bytes 32 | tf_op jit(solution)/shard_map/psum | solution.py:99
  86.4 0.2 multiply_reduce_fusion.6
  86.6 41.6 %psum.87 = f32[2]{0:T(128)S(1)} all-reduce(f32[2]{0:T(128)S(1)} %get-tuple-element.113), channel_id=1, replica_groups=mesh['row'=4,'col'=8] {'row','col'}, use_global_device_ids=true, to_apply=%region_10.11 | all-reduce | flops 2 | bytes 16 | tf_op jit(solution)/shard_map/psum | solution.py:99
  128.3 9.1 %all-gather.2 = f32[4,64,2]{1,2,0:T(2,128)S(1)} all-gather(f32[1,64,2]{1,2,0:T(2,128)S(1)} %fusion.28), channel_id=1, replica_groups=mesh['row'=4,'col'=8] {'row'}, dimensions={0}, use_global_device_ids=true | all-gather | bytes 2560 | tf_op jit(solution)/shard_map/all_gather | solution.py:107
  137.4 0.2 multiply_reduce_fusion.1
  137.7 11.8 %psum.88 = f32[2,512]{1,0:T(2,128)S(1)} all-reduce(f32[2,512]{1,0:T(2,128)S(1)} %multiply_reduce_fusion.1), channel_id=1, replica_groups=mesh['row'=4,'col'=8] {'col'}, use_global_device_ids=true, to_apply=%region_12.13 | all-reduce | flops 1024 | bytes 8192 | tf_op jit(solution)/shard_map/psum | solution.py:108
  149.7 38.5 %psum.89 = f32[2]{0:T(128)S(1)} all-reduce(f32[2]{0:T(128)S(1)} %multiply_reduce_fusion.5), channel_id=1, replica_groups=mesh['row'=4,'col'=8] {'row','col'}, use_global_device_ids=true, to_apply=%region_14.15 | all-reduce | flops 2 | bytes 16 | tf_op jit(solution)/shard_map/psum | solution.py:111
  188.2 0.2 multiply_reduce_fusion.4
  188.4 41.5 %psum.90 = f32[2]{0:T(128)S(1)} all-reduce(f32[2]{0:T(128)S(1)} %get-tuple-element.103), channel_id=1, replica_groups=mesh['row'=4,'col'=8] {'row','col'}, use_global_device_ids=true, to_apply=%region_16.17 | all-reduce | flops 2 | bytes 16 | tf_op jit(solution)/shard_map/psum | solution.py:99
  230.0 9.1 %all-gather.3 = f32[4,64,2]{1,2,0:T(2,128)S(1)} all-gather(f32[1,64,2]{1,2,0:T(2,128)S(1)} %bitcast.57), channel_id=1, replica_groups=mesh['row'=4,'col'=8] {'row'}, dimensions={0}, use_global_device_ids=true | all-gather | bytes 2560 | tf_op jit(solution)/shard_map/all_gather | solution.py:107
  239.2 0.2 multiply_reduce_fusion
  239.4 11.8 %psum.91 = f32[2,512]{1,0:T(2,128)S(1)} all-reduce(f32[2,512]{1,0:T(2,128)S(1)} %multiply_reduce_fusion), channel_id=1, replica_groups=mesh['row'=4,'col'=8] {'col'}, use_global_device_ids=true, to_apply=%region_18.19 | all-reduce | flops 1024 | bytes 8192 | tf_op jit(solution)/shard_map/psum | solution.py:108
  251.4 38.5 %psum.92 = f32[2]{0:T(128)S(1)} all-reduce(f32[2]{0:T(128)S(1)} %multiply_reduce_fusion.3), channel_id=1, replica_groups=mesh['row'=4,'col'=8] {'row','col'}, use_global_device_ids=true, to_apply=%region_20.21 | all-reduce | flops 2 | bytes 16 | tf_op jit(solution)/shard_map/psum | solution.py:111
  290.1 12.7 %psum.93 = f32[2]{0:T(128)S(1)} all-reduce(f32[2]{0:T(128)S(1)} %get-tuple-element.101), channel_id=1, replica_groups=mesh['row'=4,'col'=8] {'col'}, use_global_device_ids=true, to_apply=%region_22.23 | all-reduce | flops 2 | bytes 16 | tf_op jit(solution)/shard_map/psum | solution.py:121
  302.8 9.9 %psum.94 = f32[2]{0:T(128)S(1)} all-reduce(f32[2]{0:T(128)S(1)} %psum.93), channel_id=1, replica_groups=mesh['row'=4,'col'=8] {'row'}, use_global_device_ids=true, to_apply=%region_23.24 | all-reduce | flops 2 | bytes 16 | tf_op jit(solution)/shard_map/psum | solution.py:121
  312.7 0.6 fusion.27
  314.7 0.6 copy-done.7
  315.3 0.6 dynamic-slice
  316.7 8.8 %all-reduce.1 = f32[256]{0:T(256)S(1)} all-reduce(f32[256]{0:T(256)S(1)} %get-tuple-element.99), channel_id=2, replica_groups=mesh['row'=4,'col'=8] {'row'}, use_global_device_ids=true, to_apply=%add.1 | all-reduce | flops 256 | bytes 2048
  325.5 1.2 fusion.3
  326.7 12.0 %psum.95 = f32[3,512]{1,0:T(4,128)S(1)} all-reduce(f32[3,512]{1,0:T(4,128)S(1)} %pad_maximum_fusion), channel_id=1, replica_groups=mesh['row'=4,'col'=8] {'col'}, use_global_device_ids=true, to_apply=%region_27.28 | all-reduce | flops 1536 | bytes 12288 | tf_op jit(solution)/shard_map/psum | solution.py:127
  338.8 0.6 reshape.327
  (56 shorter events, 2.3 us)
Async XLA Ops:
  0.6 0.7 copy-start.1
  0.6 0.7 copy-start.6
  0.7 0.7 copy-start.5
  1.4 0.7 copy-start.4
  25.3 1.2 copy-start
  25.8 0.7 copy-start.2
  314.7 0.7 copy-start.7
  316.7 22.1 %copy-start.3 = (f32[1,64]{1,0:T(1,128)}, f32[1,64]{1,0:T(1,128)S(1)}, u32[]{:S(2)}) copy-start(f32[1,64]{1,0:T(1,128)S(1)} %get-tuple-element.100) | copy-start | bytes 772
